TPU v7x, 128 devices: a whole 4x4x4 slice. The times are simulated.
128 devices in a mesh: expert: 16 (over z, x), dp: 8 (over y, core).
Axes of the slice: x: 4, y: 4, z: 4, core: 2. Of those that a mesh axis runs over, the one named last changes fastest.
Arguments:
- tokens: bfloat16 [16, 480, 7168], P('expert', 'dp'), may hold values from -6 to 6
- cotangent: bfloat16 [16, 480, 7168], P('expert', 'dp'), may hold values from -1.5 to 1.5
- counts: int32 [16, 8], replicated, may hold values from 1 to 60, as said below
- w_gate: bfloat16 [16, 7168, 2048], P('expert', None, 'dp'), may hold values from -0.0625 to 0.0625
- w_up: bfloat16 [16, 7168, 2048], P('expert', None, 'dp'), may hold values from -0.0625 to 0.0625
- w_down: bfloat16 [16, 2048, 7168], P('expert', 'dp'), may hold values from -0.125 to 0.125
Outputs:
- outputs: bfloat16 [16, 480, 7168], P('expert', 'dp')
- input_grads: bfloat16 [16, 480, 7168], P('expert', 'dp')
- gate_grad: bfloat16 [16, 7168, 2048], P('expert', None, 'dp')
- up_grad: bfloat16 [16, 7168, 2048], P('expert', None, 'dp')
- down_grad: bfloat16 [16, 2048, 7168], P('expert', 'dp')
Inputs may be any that keep to these rules, and one draw needn't show every extreme that they name: For each expert e below 8, exactly one of experts e and e + 8 is hot: all its counts exceed 40 - 20 and one equals 60; every count of the other is at most 20 and one equals 20.
All inputs are finite; a program needn't handle non-finite values.
Results may differ from a plain program's by a relative error of at most 0.012.
Values may be sent and summed in bfloat16 or wider, within the bound.
No kernel may reach another device: no remote copies, remote signals or barrier semaphores. Data moves between devices by JAX's collectives and lax.ppermute only.
A program may use at most 192 MiB of HBM per device.

v0:
```python
import jax
import jax.numpy as jnp
from jax import lax
from jax.sharding import PartitionSpec as P

HOME = 40
SPILL = 20


def swapped(x, axis, distance):
    return lax.ppermute(x, axis, [(i, i ^ 1 << distance) for i in range(lax.axis_size(axis))])


def silu_slope(value):
    sigma = jax.nn.sigmoid(value)
    return sigma * (1.0 + value * (1.0 - sigma))


def contract_last(left, right):
    return lax.dot_general(
        left, right, (((1,), (1,)), ((), ())), preferred_element_type=jnp.float32
    )


def contract_first(left, right):
    return lax.dot_general(
        left, right, (((0,), (0,)), ((), ())), preferred_element_type=jnp.float32
    )


def expert_work(rows, cot_rows, gate_w, up_w, down_w):
    gate = jnp.dot(rows, gate_w, preferred_element_type=jnp.float32)
    up = jnp.dot(rows, up_w, preferred_element_type=jnp.float32)
    active = jax.nn.silu(gate)
    hidden = (active * up).astype(jnp.bfloat16)
    out_part = jnp.dot(hidden, down_w, preferred_element_type=jnp.float32)
    hidden_grad = contract_last(cot_rows, down_w)
    gate_act = (hidden_grad * up * silu_slope(gate)).astype(jnp.bfloat16)
    up_act = (hidden_grad * active).astype(jnp.bfloat16)
    in_part = contract_last(gate_act, gate_w) + contract_last(up_act, up_w)
    gate_term = contract_first(rows, gate_act)
    up_term = contract_first(rows, up_act)
    down_term = contract_first(hidden, cot_rows)
    return (out_part, in_part, gate_term, up_term, down_term)


def shards(tokens, cotangent, counts, w_gate, w_up, w_down):
    rows_in = tokens[0]
    cot_in = cotangent[0]
    gate_w = w_gate[0]
    up_w = w_up[0]
    down_w = w_down[0]
    expert_total = lax.axis_size("expert")
    expert_pos = lax.axis_index("expert")
    batch_pos = lax.axis_index("dp")
    expert_ids = jnp.arange(counts.shape[0], dtype=jnp.int32)
    batch_ids = jnp.arange(counts.shape[1], dtype=jnp.int32)
    own_counts = jnp.sum(jnp.where(expert_ids[:, None] == expert_pos, counts, 0), axis=0)
    own_total = jnp.sum(jnp.where(batch_ids == batch_pos, own_counts, 0))
    own_hot = jnp.max(own_counts) > HOME - SPILL
    slots = rows_in.shape[0]
    valid = (jnp.arange(slots, dtype=jnp.int32) < own_total)[:, None]
    masked = jnp.where(valid, rows_in, jnp.zeros_like(rows_in))
    masked_cot = jnp.where(valid, cot_in, jnp.zeros_like(cot_in))
    partner_bit = expert_total.bit_length() - 2
    border = HOME - SPILL
    got_rows, got_cot, far_gate, far_up, far_down = swapped(
        (masked[HOME:], masked_cot[HOME:], gate_w, up_w, down_w), "expert", partner_bit
    )
    region_rows = masked[border:HOME] + got_rows
    region_cot = masked_cot[border:HOME] + got_cot
    pick_gate = jnp.where(own_hot, gate_w, far_gate)
    pick_up = jnp.where(own_hot, up_w, far_up)
    pick_down = jnp.where(own_hot, down_w, far_down)
    all_home, all_region, cot_home, cot_region = (
        lax.all_gather(masked[:border], "dp", axis=0, tiled=True),
        lax.all_gather(region_rows, "dp", axis=0, tiled=True),
        lax.all_gather(masked_cot[:border], "dp", axis=0, tiled=True),
        lax.all_gather(region_cot, "dp", axis=0, tiled=True),
    )
    home_res = expert_work(all_home, cot_home, gate_w, up_w, down_w)
    region_res = expert_work(all_region, cot_region, pick_gate, pick_up, pick_down)
    home_out, region_sum_out, home_in, region_sum_in = (
        lax.psum_scatter(
            home_res[0].astype(jnp.bfloat16), "dp", scatter_dimension=0, tiled=True
        ).astype(jnp.float32),
        lax.psum_scatter(
            region_res[0].astype(jnp.bfloat16), "dp", scatter_dimension=0, tiled=True
        ).astype(jnp.float32),
        lax.psum_scatter(
            home_res[1].astype(jnp.bfloat16), "dp", scatter_dimension=0, tiled=True
        ).astype(jnp.float32),
        lax.psum_scatter(
            region_res[1].astype(jnp.bfloat16), "dp", scatter_dimension=0, tiled=True
        ).astype(jnp.float32),
    )
    region_out = region_sum_out.astype(jnp.bfloat16)
    region_in = region_sum_in.astype(jnp.bfloat16)
    blank = jnp.zeros_like(region_out)
    back_out, back_in = swapped(
        (jnp.where(own_hot, blank, region_out), jnp.where(own_hot, blank, region_in)),
        "expert",
        partner_bit,
    )
    outputs = jnp.concatenate(
        [home_out.astype(jnp.bfloat16), jnp.where(own_hot, region_out, blank), back_out], axis=0
    )
    input_grads = jnp.concatenate(
        [home_in.astype(jnp.bfloat16), jnp.where(own_hot, region_in, blank), back_in], axis=0
    )
    kept = [home_res[k] + jnp.where(own_hot, region_res[k], 0.0) for k in (2, 3, 4)]
    sending = [jnp.where(own_hot, 0.0, region_res[k]).astype(jnp.bfloat16) for k in (2, 3, 4)]
    got_gate, got_up, got_down = swapped(
        (sending[0], sending[1], sending[2]), "expert", partner_bit
    )
    gate_grad = (kept[0] + got_gate.astype(jnp.float32)).astype(jnp.bfloat16)
    up_grad = (kept[1] + got_up.astype(jnp.float32)).astype(jnp.bfloat16)
    down_grad = (kept[2] + got_down.astype(jnp.float32)).astype(jnp.bfloat16)
    return (outputs[None], input_grads[None], gate_grad[None], up_grad[None], down_grad[None])


def solution(mesh):
    placed = (
        P("expert", "dp", None),
        P("expert", "dp", None),
        P(),
        P("expert", None, "dp"),
        P("expert", None, "dp"),
        P("expert", "dp", None),
    )
    return jax.shard_map(
        shards,
        mesh=mesh,
        in_specs=placed,
        out_specs=(
            P("expert", "dp", None),
            P("expert", "dp", None),
            P("expert", None, "dp"),
            P("expert", None, "dp"),
            P("expert", "dp", None),
        ),
        check_vma=False,
    )
```

profile of v0, /device:TPU:0, one launch (start us, length us, event | category | flops | bytes accessed | tf_op | source)
XLA Modules:
  0.0 693.8 jit_solution(14175474029074275268)
XLA Ops:
  7.2 0.8 select_reduce_fusion
  9.3 1.6 bitcast_select_fusion
  12.7 4.1 collective-permute-start.5
  16.8 8.1 %collective-permute-done.5 = bf16[20,7168]{1,0:T(8,128)(2,1)S(1)} collective-permute-done((bf16[20,7168]{1,0:T(8,128)(2,1)S(1)}, bf16[20,7168]{1,0:T(8,128)(2,1)S(1)}, u32[]{:S(2)}, u32[]{:S(2)}) %collective-permute-start.5) | collective-permute-done | bytes 286752 | tf_op jit(solution)/shard_map/ppermute | solution.py:11
  24.8 0.8 fusion.13
  25.7 3.3 collective-permute-start
  29.1 7.5 %collective-permute-done = bf16[20,7168]{1,0:T(8,128)(2,1)S(1)} collective-permute-done((bf16[20,7168]{1,0:T(8,128)(2,1)S(1)}, bf16[20,7168]{1,0:T(8,128)(2,1)S(1)}, u32[]{:S(2)}, u32[]{:S(2)}) %collective-permute-start) | collective-permute-done | bytes 286752 | tf_op jit(solution)/shard_map/ppermute | solution.py:11
  36.6 0.8 fusion.14
  37.4 3.0 collective-permute-start.3
  41.0 3.0 collective-permute-start.1
  46.0 4.1 reshape.24
  50.1 19.3 %all-gather.9.cloned.1.call-done = bf16[8,20,7168]{2,1,0:T(8,128)(2,1)} async-done(((bf16[1,20,7168]{2,1,0:T(8,128)(2,1)}), bf16[8,20,7168]{2,1,0:T(8,128)(2,1)}) %all-gather.9.cloned.1.call-update) | async-done | bytes 2293776 | tf_op jit(solution)/shard_map/all_gather | solution.py:76
  69.5 2.7 reshape.20
  72.2 3.0 fusion.26
  75.4 0.8 fusion.32
  76.2 1.2 copy-done.6
  78.1 1.4 multiply_convert_fusion.2
  79.5 2.2 convolution_convert_fusion.1
  81.7 1.4 fusion.29
  83.1 0.9 copy-done.4
  84.0 2.8 fusion.4
  86.8 11.6 %all-gather.15.cloned.1.call-done = bf16[8,20,7168]{2,1,0:T(8,128)(2,1)} async-done(((bf16[1,20,7168]{2,1,0:T(8,128)(2,1)}), bf16[8,20,7168]{2,1,0:T(8,128)(2,1)}) %all-gather.15.cloned.1.call-update) | async-done | bytes 2293776 | tf_op jit(solution)/shard_map/all_gather | solution.py:79
  98.4 4.1 reshape.26
  102.5 24.7 %all-gather.11.cloned.1.call-done = bf16[8,20,7168]{2,1,0:T(8,128)(2,1)} async-done(((bf16[1,20,7168]{2,1,0:T(8,128)(2,1)}), bf16[8,20,7168]{2,1,0:T(8,128)(2,1)}) %all-gather.11.cloned.1.call-update) | async-done | bytes 2293776 | tf_op jit(solution)/shard_map/all_gather | solution.py:77
  127.2 4.1 reshape.22
  131.4 4.1 fusion.12
  135.5 64.7 %collective-permute-done.2 = bf16[7168,256]{1,0:T(8,128)(2,1)} collective-permute-done((bf16[7168,256]{1,0:T(8,128)(2,1)}, bf16[7168,256]{1,0:T(8,128)(2,1)}, u32[]{:S(2)}, u32[]{:S(2)}) %collective-permute-start.2) | collective-permute-done | bytes 3670048 | tf_op jit(solution)/shard_map/ppermute | solution.py:11
  200.2 1.0 fusion.11
  201.2 75.1 %collective-permute-done.1 = bf16[7168,256]{1,0:T(8,128)(2,1)} collective-permute-done((bf16[7168,256]{1,0:T(8,128)(2,1)}, bf16[7168,256]{1,0:T(8,128)(2,1)}, u32[]{:S(2)}, u32[]{:S(2)}) %collective-permute-start.1) | collective-permute-done | bytes 3670048 | tf_op jit(solution)/shard_map/ppermute | solution.py:11
  276.3 1.1 multiply_convert_fusion.1
  277.4 2.5 convolution_convert_fusion
  279.9 1.4 fusion.10
  281.4 3.1 fusion.5
  284.5 67.3 %fusion.34 = (bf16[24,7168]{1,0:T(8,128)(2,1)S(1)}, bf16[24,7168]{1,0:T(8,128)(2,1)}, bf16[24,7168]{1,0:T(8,128)(2,1)}, bf16[24,7168]{1,0:T(8,128)(2,1)S(1)}) fusion(bf16[160,7168]{1,0:T(8,128)(2,1)} %convolution_convert_fusion, bf16[160,7168]{1,0:T(8,128)(2,1)} %convolution_convert_fusion.1, bf16[160,7168]{1,0:T(8,128)(2,1)} %fusion.5, ...), kind=kCustom, calls=%all-reduce-scatter.4 | all-reduce-scatter fusion | flops 5505025 | bytes 10551808
  351.8 1.3 collective-permute-start.12
  353.1 1.6 slice.30
  354.7 3.6 collective-permute-start.10
  358.3 7.1 %select_convert_fusion = (bf16[256,7168]{1,0:T(8,128)(2,1)}, f32[256,7168]{1,0:T(8,128)}) fusion(pred[]{:T(512)S(6)} %gt.3, bf16[160,256]{1,0:T(8,128)(2,1)} %copy-done.12, bf16[160,7168]{1,0:T(8,128)(2,1)} %reshape.26), kind=kOutput, calls=%fused_computation.10 | convolution fusion | flops 589037568 | bytes 13385729 | tf_op jit(solution)/shard_map/dot_general | solution.py:26
  365.4 5.5 select_convert_fusion.2
  370.8 2.6 collective-permute-start.13
  373.5 5.3 select_convert_fusion.1
  378.8 2.3 collective-permute-start.16
  381.2 1.6 slice.33
  382.7 4.0 collective-permute-start.14
  387.4 1.9 collective-permute-start.15
  390.0 1.9 collective-permute-start.17
  391.9 7.9 %concatenate.9 = bf16[52,7168]{1,0:T(8,128)(2,1)S(1)} concatenate(bf16[4,7168]{1,0:T(4,128)(2,1)} %copy-done.19, bf16[24,7168]{1,0:T(8,128)(2,1)} %copy-done.11, bf16[24,7168]{1,0:T(8,128)(2,1)} %copy-done.10), dimensions={0} | concatenate | bytes 1490944
  399.8 1.0 broadcast_select_fusion.12
  400.8 1.9 collective-permute-start.11
  402.7 11.0 %collective-permute-start.9 = (bf16[256,7168]{1,0:T(8,128)(2,1)}, bf16[256,7168]{1,0:T(8,128)(2,1)}, u32[]{:S(2)}, u32[]{:S(2)}) collective-permute-start(bf16[256,7168]{1,0:T(8,128)(2,1)} %get-tuple-element.35), channel_id=1, source_target_pairs={{0,64},{8,72},{16,80},{24,88},{32,96},{40,104},{48,112},{56,120},{... | collective-permute-start | bytes 11010056 | tf_op jit(solution)/shard_map/ppermute | solution.py:11
  413.7 7.9 %concatenate.11 = bf16[52,7168]{1,0:T(8,128)(2,1)S(1)} concatenate(bf16[4,7168]{1,0:T(4,128)(2,1)} %collective-permute-done.17, bf16[24,7168]{1,0:T(8,128)(2,1)} %collective-permute-done.16, bf16[24,7168]{1,0:T(8,128)(2,1)} %get-tuple-element.13), dimensions={0} | concatenate | bytes 1490944
  421.6 1.0 broadcast_select_fusion.10
  422.6 3.5 collective-permute-start.8
  426.1 7.9 %concatenate.8 = bf16[52,7168]{1,0:T(8,128)(2,1)S(1)} concatenate(bf16[4,7168]{1,0:T(4,128)(2,1)} %collective-permute-done.11, bf16[24,7168]{1,0:T(8,128)(2,1)} %collective-permute-done.10, bf16[24,7168]{1,0:T(8,128)(2,1)} %get-tuple-element.12), dimensions={0} | concatenate | bytes 1490944
  434.2 3.4 collective-permute-start.6
  437.6 9.5 %concatenate.10 = bf16[52,7168]{1,0:T(8,128)(2,1)} concatenate(bf16[4,7168]{1,0:T(4,128)(2,1)} %collective-permute-done.15, bf16[24,7168]{1,0:T(8,128)(2,1)} %collective-permute-done.14, bf16[24,7168]{1,0:T(8,128)(2,1)S(1)} %get-tuple-element.14), dimensions={0} | concatenate | bytes 1490944
  447.2 1.3 constant_dynamic-slice_fusion
  448.5 210.4 %collective-permute-done.4 = bf16[20,7168]{1,0:T(8,128)(2,1)} collective-permute-done((bf16[20,7168]{1,0:T(8,128)(2,1)}, bf16[20,7168]{1,0:T(8,128)(2,1)}, u32[]{:S(2)}, u32[]{:S(2)}) %collective-permute-start.4) | collective-permute-done | bytes 286752 | tf_op jit(solution)/shard_map/ppermute | solution.py:11
  658.8 2.2 maximum_bitcast_fusion
  661.0 4.2 collective-permute-done.6
  665.2 2.3 maximum_bitcast_fusion.1
  667.6 7.9 %fusion.6 = bf16[1,256,7168]{2,1,0:T(8,128)(2,1)} fusion(bf16[256,7168]{1,0:T(8,128)(2,1)} %collective-permute-done.9, f32[256,7168]{1,0:T(8,128)} %get-tuple-element.36, bf16[160,256]{1,0:T(8,128)(2,1)S(1)} %get-tuple-element.25, bf16[160,7168]{1,0:T(8,128)(2,1)S(1)} %copy-done.9, pred[]{:T(512)S(6)} %gt.3), kind=kOutput, calls=%fused_computation.11 | convolution fusion | flops 596377600 | bytes 17055744 | tf_op jit(solution)/shard_map/dot_general | solution.py:26
  675.5 5.9 fusion.8
  681.4 5.8 fusion.7
  (83 shorter events, 7.0 us)
Async XLA Ops:
  7.2 38.8 %all-gather.13.cloned.1.call-start = ((), (), s32[]{:S(2)}) async-start(), calls=%async_computation.2 | async-start | bytes 3096576 | tf_op jit(solution)/shard_map/all_gather | solution.py:78
  11.0 33.0 %copy-start.20 = (u32[128]{0:T(128)S(1)}, u32[128]{0:T(128)}, u32[]{:S(2)}) copy-start(u32[128]{0:T(128)} %constant.32) | copy-start | bytes 1540
  11.8 57.7 %all-gather.9.cloned.1.call-start = ((), (), s32[]{:S(2)}) async-start(), calls=%async_computation | async-start | bytes 3096576 | tf_op jit(solution)/shard_map/all_gather | solution.py:76
  12.6 85.8 %all-gather.15.cloned.1.call-start = ((), (), s32[]{:S(2)}) async-start(), calls=%async_computation.3 | async-start | bytes 3096576 | tf_op jit(solution)/shard_map/all_gather | solution.py:79
  12.7 12.1 %collective-permute-start.5 = (bf16[20,7168]{1,0:T(8,128)(2,1)S(1)}, bf16[20,7168]{1,0:T(8,128)(2,1)S(1)}, u32[]{:S(2)}, u32[]{:S(2)}) collective-permute-start(bf16[20,7168]{1,0:T(8,128)(2,1)S(1)} %get-tuple-element.16), channel_id=1, source_target_pairs={{0,64},{8,72},{16,80},{24,88},{32,96},{40,104},{48,112},{56,120},{... | collective-permute-start | bytes 860168 | tf_op jit(solution)/shard_map/ppermute | solution.py:11
  25.7 101.5 %all-gather.11.cloned.1.call-start = ((), (), s32[]{:S(2)}) async-start(), calls=%async_computation.1 | async-start | bytes 3096576 | tf_op jit(solution)/shard_map/all_gather | solution.py:77
  25.7 10.8 %collective-permute-start = (bf16[20,7168]{1,0:T(8,128)(2,1)S(1)}, bf16[20,7168]{1,0:T(8,128)(2,1)S(1)}, u32[]{:S(2)}, u32[]{:S(2)}) collective-permute-start(bf16[20,7168]{1,0:T(8,128)(2,1)S(1)} %get-tuple-element.18), channel_id=1, source_target_pairs={{0,64},{8,72},{16,80},{24,88},{32,96},{40,104},{48,112},{56,120},{... | collective-permute-start | bytes 860168 | tf_op jit(solution)/shard_map/ppermute | solution.py:11
  37.4 93.9 %collective-permute-start.3 = (bf16[256,7168]{1,0:T(8,128)(2,1)}, bf16[256,7168]{1,0:T(8,128)(2,1)}, u32[]{:S(2)}, u32[]{:S(2)}) collective-permute-start(bf16[256,7168]{1,0:T(8,128)(2,1)} %bitcast.105), channel_id=1, source_target_pairs={{0,64},{8,72},{16,80},{24,88},{32,96},{40,104},{48,112},{56,120},{... | collective-permute-start | bytes 11010056 | tf_op jit(solution)/shard_map/ppermute | solution.py:11
  40.5 159.7 %collective-permute-start.2 = (bf16[7168,256]{1,0:T(8,128)(2,1)}, bf16[7168,256]{1,0:T(8,128)(2,1)}, u32[]{:S(2)}, u32[]{:S(2)}) collective-permute-start(bf16[7168,256]{1,0:T(8,128)(2,1)} %bitcast.104), channel_id=1, source_target_pairs={{0,64},{8,72},{16,80},{24,88},{32,96},{40,104},{48,112},{56,120},{... | collective-permute-start | bytes 11010056 | tf_op jit(solution)/shard_map/ppermute | solution.py:11
  41.0 235.2 %collective-permute-start.1 = (bf16[7168,256]{1,0:T(8,128)(2,1)}, bf16[7168,256]{1,0:T(8,128)(2,1)}, u32[]{:S(2)}, u32[]{:S(2)}) collective-permute-start(bf16[7168,256]{1,0:T(8,128)(2,1)} %bitcast.103), channel_id=1, source_target_pairs={{0,64},{8,72},{16,80},{24,88},{32,96},{40,104},{48,112},{56,120},{... | collective-permute-start | bytes 11010056 | tf_op jit(solution)/shard_map/ppermute | solution.py:11
  72.2 3.1 copy-start.2
  75.4 2.0 copy-start.6
  75.4 2.8 copy-start.8
  79.5 2.2 copy-start.13
  79.5 3.5 copy-start.17
  81.7 2.3 copy-start.4
  131.3 68.8 %copy-start = (bf16[160,7168]{1,0:T(8,128)(2,1)S(1)}, bf16[160,7168]{1,0:T(8,128)(2,1)}, u32[]{:S(2)}) copy-start(bf16[160,7168]{1,0:T(8,128)(2,1)} %reshape.22) | copy-start | bytes 6881284
  131.3 68.8 %copy-start.5 = (bf16[1,7168,256]{2,1,0:T(8,128)(2,1)S(1)}, bf16[1,7168,256]{2,1,0:T(8,128)(2,1)}, u32[]{:S(2)}) copy-start(bf16[1,7168,256]{2,1,0:T(8,128)(2,1)} %param.10) | copy-start | bytes 11010052
  135.4 140.8 %copy-start.3 = (bf16[1,7168,256]{2,1,0:T(8,128)(2,1)S(1)}, bf16[1,7168,256]{2,1,0:T(8,128)(2,1)}, u32[]{:S(2)}) copy-start(bf16[1,7168,256]{2,1,0:T(8,128)(2,1)} %param.9) | copy-start | bytes 11010052
  201.2 76.2 %copy-start.7 = (bf16[1,256,7168]{2,1,0:T(8,128)(2,1)S(1)}, bf16[1,256,7168]{2,1,0:T(8,128)(2,1)}, u32[]{:S(2)}) copy-start(bf16[1,256,7168]{2,1,0:T(8,128)(2,1)} %param.11) | copy-start | bytes 11010052
  277.4 2.6 copy-start.12
  277.4 4.0 copy-start.15
  351.8 13.6 %copy-start.10 = (bf16[24,7168]{1,0:T(8,128)(2,1)}, bf16[24,7168]{1,0:T(8,128)(2,1)S(1)}, u32[]{:S(2)}) copy-start(bf16[24,7168]{1,0:T(8,128)(2,1)S(1)} %get-tuple-element.11) | copy-start | bytes 1032196
  351.8 37.5 %collective-permute-start.12 = (bf16[24,7168]{1,0:T(8,128)(2,1)S(1)}, bf16[24,7168]{1,0:T(8,128)(2,1)S(1)}, u32[]{:S(2)}, u32[]{:S(2)}) collective-permute-start(bf16[24,7168]{1,0:T(8,128)(2,1)S(1)} %get-tuple-element.11), channel_id=1, source_target_pairs={{0,1},{1,2},{2,3},{3,4},{4,5},{5,6},{6,7},{8,9},{9,10},{10,11},{11... | collective-permute-start | bytes 1032200
  354.7 10.7 %copy-start.1 = (bf16[160,7168]{1,0:T(8,128)(2,1)S(1)}, bf16[160,7168]{1,0:T(8,128)(2,1)}, u32[]{:S(2)}) copy-start(bf16[160,7168]{1,0:T(8,128)(2,1)} %reshape.22) | copy-start | bytes 6881284
  354.7 10.7 %copy-start.16 = (bf16[160,256]{1,0:T(8,128)(2,1)S(1)}, bf16[160,256]{1,0:T(8,128)(2,1)}, u32[]{:S(2)}) copy-start(bf16[160,256]{1,0:T(8,128)(2,1)} %copy-done.15) | copy-start | bytes 245764
  354.7 67.9 %collective-permute-start.10 = (bf16[24,7168]{1,0:T(8,128)(2,1)}, bf16[24,7168]{1,0:T(8,128)(2,1)}, u32[]{:S(2)}, u32[]{:S(2)}) collective-permute-start(bf16[24,7168]{1,0:T(8,128)(2,1)} %get-tuple-element.12), channel_id=1, source_target_pairs={{0,1},{1,2},{2,3},{3,4},{4,5},{5,6},{6,7},{8,9},{9,10},{10,11},{11... | collective-permute-start | bytes 1032200
  370.8 16.6 %collective-permute-start.13 = (bf16[4,7168]{1,0:T(4,128)(2,1)S(1)}, bf16[4,7168]{1,0:T(4,128)(2,1)S(1)}, u32[]{:S(2)}, u32[]{:S(2)}) collective-permute-start(bf16[4,7168]{1,0:T(4,128)(2,1)S(1)} %slice.31), channel_id=1, source_target_pairs={{0,2},{1,3},{2,4},{3,5},{4,6},{5,7},{8,10},{9,11},{10,12},{11,13},... | collective-permute-start | bytes 172040
  378.8 23.9 %collective-permute-start.16 = (bf16[24,7168]{1,0:T(8,128)(2,1)}, bf16[24,7168]{1,0:T(8,128)(2,1)}, u32[]{:S(2)}, u32[]{:S(2)}) collective-permute-start(bf16[24,7168]{1,0:T(8,128)(2,1)} %get-tuple-element.13), channel_id=1, source_target_pairs={{0,1},{1,2},{2,3},{3,4},{4,5},{5,6},{6,7},{8,9},{9,10},{10,11},{11... | collective-permute-start | bytes 1032200
  382.7 51.5 %collective-permute-start.14 = (bf16[24,7168]{1,0:T(8,128)(2,1)S(1)}, bf16[24,7168]{1,0:T(8,128)(2,1)}, u32[]{:S(2)}, u32[]{:S(2)}) collective-permute-start(bf16[24,7168]{1,0:T(8,128)(2,1)S(1)} %get-tuple-element.14), channel_id=1, source_target_pairs={{0,1},{1,2},{2,3},{3,4},{4,5},{5,6},{6,7},{8,9},{9,10},{10,11},{11... | collective-permute-start | bytes 1032200
  387.4 1.9 copy-start.19
  387.4 46.6 %collective-permute-start.15 = (bf16[4,7168]{1,0:T(4,128)(2,1)}, bf16[4,7168]{1,0:T(4,128)(2,1)}, u32[]{:S(2)}, u32[]{:S(2)}) collective-permute-start(bf16[4,7168]{1,0:T(4,128)(2,1)} %slice.32), channel_id=1, source_target_pairs={{0,2},{1,3},{2,4},{3,5},{4,6},{5,7},{8,10},{9,11},{10,12},{11,13},... | collective-permute-start | bytes 172040
  389.3 0.7 copy-start.11
  390.0 10.8 %collective-permute-start.17 = (bf16[4,7168]{1,0:T(4,128)(2,1)}, bf16[4,7168]{1,0:T(4,128)(2,1)}, u32[]{:S(2)}, u32[]{:S(2)}) collective-permute-start(bf16[4,7168]{1,0:T(4,128)(2,1)} %slice.33), channel_id=1, source_target_pairs={{0,2},{1,3},{2,4},{3,5},{4,6},{5,7},{8,10},{9,11},{10,12},{11,13},... | collective-permute-start | bytes 172040
  400.8 21.8 %collective-permute-start.11 = (bf16[4,7168]{1,0:T(4,128)(2,1)}, bf16[4,7168]{1,0:T(4,128)(2,1)}, u32[]{:S(2)}, u32[]{:S(2)}) collective-permute-start(bf16[4,7168]{1,0:T(4,128)(2,1)} %slice.30), channel_id=1, source_target_pairs={{0,2},{1,3},{2,4},{3,5},{4,6},{5,7},{8,10},{9,11},{10,12},{11,13},... | collective-permute-start | bytes 172040
  402.7 264.8 %collective-permute-start.9 = (bf16[256,7168]{1,0:T(8,128)(2,1)}, bf16[256,7168]{1,0:T(8,128)(2,1)}, u32[]{:S(2)}, u32[]{:S(2)}) collective-permute-start(bf16[256,7168]{1,0:T(8,128)(2,1)} %get-tuple-element.35), channel_id=1, source_target_pairs={{0,64},{8,72},{16,80},{24,88},{32,96},{40,104},{48,112},{56,120},{... | collective-permute-start | bytes 11010056 | tf_op jit(solution)/shard_map/ppermute | solution.py:11
  422.6 252.8 %collective-permute-start.7 = (bf16[7168,256]{1,0:T(8,128)(2,1)}, bf16[7168,256]{1,0:T(8,128)(2,1)}, u32[]{:S(2)}, u32[]{:S(2)}) collective-permute-start(bf16[7168,256]{1,0:T(8,128)(2,1)} %get-tuple-element.31), channel_id=1, source_target_pairs={{0,64},{8,72},{16,80},{24,88},{32,96},{40,104},{48,112},{56,120},{... | collective-permute-start | bytes 11010056 | tf_op jit(solution)/shard_map/ppermute | solution.py:11
  422.6 258.8 %collective-permute-start.8 = (bf16[7168,256]{1,0:T(8,128)(2,1)}, bf16[7168,256]{1,0:T(8,128)(2,1)}, u32[]{:S(2)}, u32[]{:S(2)}) collective-permute-start(bf16[7168,256]{1,0:T(8,128)(2,1)} %get-tuple-element.33), channel_id=1, source_target_pairs={{0,64},{8,72},{16,80},{24,88},{32,96},{40,104},{48,112},{56,120},{... | collective-permute-start | bytes 11010056 | tf_op jit(solution)/shard_map/ppermute | solution.py:11
  434.0 224.8 %collective-permute-start.4 = (bf16[20,7168]{1,0:T(8,128)(2,1)}, bf16[20,7168]{1,0:T(8,128)(2,1)}, u32[]{:S(2)}, u32[]{:S(2)}) collective-permute-start(bf16[20,7168]{1,0:T(8,128)(2,1)} %get-tuple-element.22), channel_id=1, source_target_pairs={{0,64},{8,72},{16,80},{24,88},{32,96},{40,104},{48,112},{56,120},{... | collective-permute-start | bytes 860168 | tf_op jit(solution)/shard_map/ppermute | solution.py:11
  434.2 231.0 %collective-permute-start.6 = (bf16[20,7168]{1,0:T(8,128)(2,1)}, bf16[20,7168]{1,0:T(8,128)(2,1)}, u32[]{:S(2)}, u32[]{:S(2)}) collective-permute-start(bf16[20,7168]{1,0:T(8,128)(2,1)} %get-tuple-element.20), channel_id=1, source_target_pairs={{0,64},{8,72},{16,80},{24,88},{32,96},{40,104},{48,112},{56,120},{... | collective-permute-start | bytes 860168 | tf_op jit(solution)/shard_map/ppermute | solution.py:11
  447.1 220.4 %copy-start.9 = (bf16[160,7168]{1,0:T(8,128)(2,1)S(1)}, bf16[160,7168]{1,0:T(8,128)(2,1)}, u32[]{:S(2)}) copy-start(bf16[160,7168]{1,0:T(8,128)(2,1)} %reshape.24) | copy-start | bytes 6881284
  665.2 10.2 %slice-start.2 = ((s8[7340032]{0:T(1024)(128)(4,1)}), s8[4194304]{0:T(1024)(128)(4,1)S(1)}, s32[]{:S(2)}) async-start(s8[7340032]{0:T(1024)(128)(4,1)} %bitcast.101), calls=%async_computation.6 | async-start | bytes 8388608
  667.5 7.9 %slice-start.3 = ((s8[7340032]{0:T(1024)(128)(4,1)}), s8[3145728]{0:T(1024)(128)(4,1)S(1)}, s32[]{:S(2)}) async-start(s8[7340032]{0:T(1024)(128)(4,1)} %bitcast.101), calls=%async_computation.7 | async-start | bytes 6291456
  667.5 7.9 %copy-start.14 = (bf16[160,256]{1,0:T(8,128)(2,1)S(1)}, bf16[160,256]{1,0:T(8,128)(2,1)}, u32[]{:S(2)}) copy-start(bf16[160,256]{1,0:T(8,128)(2,1)} %copy-done.13) | copy-start | bytes 245764
  667.6 13.9 %slice-start = ((s8[7340032]{0:T(1024)(128)(4,1)}), s8[4194304]{0:T(1024)(128)(4,1)S(1)}, s32[]{:S(2)}) async-start(s8[7340032]{0:T(1024)(128)(4,1)} %bitcast.99), calls=%async_computation.4 | async-start | bytes 8388608
  675.4 6.0 slice-start.1
  675.5 6.0 copy-start.18
Sparse Core Ops, SparseCore 0:
  11.9 28.5 all-gather.12
  42.8 26.6 all-gather.8
  71.7 26.6 all-gather.14
  100.5 26.6 all-gather.10
where the time goes:
time: 696 us; the launch traced here: 694 us
  waiting for transfers between devices  426 us (61%)
  blocking collectives  67.3 us (10%)
  matrix products  62.1 us (9%)
  local copies, waits for them, and re-layouts  59.5 us (9%)
  starting transfers between devices  51.8 us (7%)
  between operations  15.4 us (2%)
  other arithmetic  12 us (2%)
    ppermute x10, waiting for transfers between devices, swapped(): lax.ppermute(x, axis, [(i, i ^ 1 << distance) for i in range(lax.axis_siz...  370 us
    unnamed x1, blocking collectives  67.3 us
    unnamed x67, local copies, waits for them, and re-layouts  59.5 us
    dot_general x6, matrix products, contract_first(): lax.dot_general(left, right, (((0,), (0,)), ((), ())), preferred_element_...  37.5 us
    ppermute x10, starting transfers between devices, swapped(): lax.ppermute(x, axis, [(i, i ^ 1 << distance) for i in range(lax.axis_siz...  32.1 us
    all_gather x1, waiting for transfers between devices, shards(): lax.all_gather(region_rows, 'dp', axis=0, tiled=True)  24.7 us
    unnamed x8, starting transfers between devices  19.6 us
    all_gather x1, waiting for transfers between devices, shards(): lax.all_gather(masked[:border], 'dp', axis=0, tiled=True)  19.3 us
  transfers between devices with their start and end apart: 22, of which 9 were waited for; matrix products, arithmetic and copies ran while one was open for 16% of the time, Pallas kernels for 0%

commit v1 on v0

--- a/solution.py
+++ b/solution.py
@@ -45,6 +45,13 @@
 
 
 def shards(tokens, cotangent, counts, w_gate, w_up, w_down):
+
+    def move_array(piece_in):
+        ready = lax.axis_size("dp")
+        vec_out = jnp.stack(ready * [piece_in], axis=0)
+        q_next = jnp.concatenate(lax.all_to_all(vec_out, "dp", split_axis=0, concat_axis=0), axis=0)
+        return q_next
+
     rows_in = tokens[0]
     cot_in = cotangent[0]
     gate_w = w_gate[0]
@@ -73,7 +80,7 @@
     pick_up = jnp.where(own_hot, up_w, far_up)
     pick_down = jnp.where(own_hot, down_w, far_down)
     all_home, all_region, cot_home, cot_region = (
-        lax.all_gather(masked[:border], "dp", axis=0, tiled=True),
+        move_array(masked[:border]),
         lax.all_gather(region_rows, "dp", axis=0, tiled=True),
         lax.all_gather(masked_cot[:border], "dp", axis=0, tiled=True),
         lax.all_gather(region_cot, "dp", axis=0, tiled=True),

time: 696 us -> 696 us (level)
  waiting for transfers between devices: 426 us -> 419 us
    all_to_all x0 -> x1, waiting for transfers between devices: none -> 28.5 us  [move_array(): lax.all_to_all(vec_out, 'dp', split_axis=0, concat_axis=0)]
    all_gather x1 -> x0, waiting for transfers between devices: 19.3 us -> none  [shards(): lax.all_gather(masked[:border], 'dp', axis=0, tiled=True)]
    all_gather x1, waiting for transfers between devices: 24.7 us -> 8.97 us  [shards(): lax.all_gather(region_rows, 'dp', axis=0, tiled=True)]
    all_gather x1, waiting for transfers between devices: 11.6 us -> 0.01 us  [shards(): lax.all_gather(region_cot, 'dp', axis=0, tiled=True)]
    ppermute x10, waiting for transfers between devices: 370 us -> 381 us  [swapped(): lax.ppermute(x, axis, [(i, i ^ 1 << distance) for i in range(lax.axis_siz...]
    unnamed x67 -> x65, local copies, waits for them, and re-layouts: 59.5 us -> 54.7 us
  transfers between devices with their start and end apart: 22 -> 22, of which waited for: 9 -> 9; matrix products, arithmetic and copies ran while one was open for 16% -> 17% of each run, Pallas kernels for 0% -> 0%
where the time goes in v1:
time: 696 us; the launch traced here: 693 us
  waiting for transfers between devices  419 us (60%)
  blocking collectives  67.1 us (10%)
  matrix products  65 us (9%)
  local copies, waits for them, and re-layouts  59.3 us (9%)
  starting transfers between devices  55.5 us (8%)
  between operations  15.3 us (2%)
  other arithmetic  12 us (2%)
    ppermute x10, waiting for transfers between devices, swapped(): lax.ppermute(x, axis, [(i, i ^ 1 << distance) for i in range(lax.axis_siz...  381 us
    unnamed x1, blocking collectives  67.1 us
    unnamed x65, local copies, waits for them, and re-layouts  54.7 us
    dot_general x6, matrix products, contract_first(): lax.dot_general(left, right, (((0,), (0,)), ((), ())), preferred_element_...  37.5 us
    ppermute x10, starting transfers between devices, swapped(): lax.ppermute(x, axis, [(i, i ^ 1 << distance) for i in range(lax.axis_siz...  31.2 us
    all_to_all x1, waiting for transfers between devices, move_array(): lax.all_to_all(vec_out, 'dp', split_axis=0, concat_axis=0)  28.5 us
    unnamed x8, starting transfers between devices  19.6 us
    dot_general x6, matrix products, contract_last(): lax.dot_general(left, right, (((1,), (1,)), ((), ())), preferred_element_...  16.8 us
  transfers between devices with their start and end apart: 22, of which 9 were waited for; matrix products, arithmetic and copies ran while one was open for 17% of the time, Pallas kernels for 0%

profile of v1, /device:TPU:0, one launch (start us, length us, event | category | flops | bytes accessed | tf_op | source)
XLA Modules:
  0.0 693.0 jit_solution(18427171785911707112)
XLA Ops:
  7.2 0.8 select_reduce_fusion
  9.3 1.6 bitcast_select_fusion
  11.8 4.1 collective-permute-start.5
  15.9 8.1 %collective-permute-done.5 = bf16[20,7168]{1,0:T(8,128)(2,1)S(1)} collective-permute-done((bf16[20,7168]{1,0:T(8,128)(2,1)S(1)}, bf16[20,7168]{1,0:T(8,128)(2,1)S(1)}, u32[]{:S(2)}, u32[]{:S(2)}) %collective-permute-start.5) | collective-permute-done | bytes 286752 | tf_op jit(solution)/shard_map/ppermute | solution.py:11
  24.0 0.8 fusion.13
  24.9 3.3 collective-permute-start
  28.2 1.8 stack.2
  30.0 4.6 all-to-all-start
  34.7 1.0 collective-permute-done
  35.7 0.8 fusion.14
  36.6 3.0 collective-permute-start.3
  40.2 3.0 collective-permute-start.1
  44.9 28.5 %all-to-all-done = bf16[8,20,7168]{2,1,0:T(8,128)(2,1)} async-done(((bf16[8,20,7168]{2,1,0:T(8,128)(2,1)}), bf16[8,20,7168]{2,1,0:T(8,128)(2,1)}, u32[]{:S(2)}, u32[]{:S(2)}) %all-to-all-start) | async-done | bytes 2293792 | tf_op jit(solution)/shard_map/all_to_all | solution.py:52
  73.4 2.8 reshape.24
  76.2 3.0 fusion.26
  80.3 4.2 reshape.28
  84.5 4.3 multiply_convert_fusion.2
  88.8 2.2 convolution_convert_fusion.1
  91.7 1.4 fusion.29
  93.1 0.9 copy-done.5
  93.9 2.8 fusion.4
  96.7 4.2 reshape.30
  100.9 9.0 %all-gather.7.cloned.1.call-done = bf16[8,20,7168]{2,1,0:T(8,128)(2,1)} async-done(((bf16[1,20,7168]{2,1,0:T(8,128)(2,1)}), bf16[8,20,7168]{2,1,0:T(8,128)(2,1)}) %all-gather.7.cloned.1.call-update) | async-done | bytes 2293776 | tf_op jit(solution)/shard_map/all_gather | solution.py:84
  109.8 4.1 reshape.26
  114.0 6.7 collective-permute-done.3
  120.7 3.9 fusion.12
  124.6 74.7 %collective-permute-done.2 = bf16[7168,256]{1,0:T(8,128)(2,1)} collective-permute-done((bf16[7168,256]{1,0:T(8,128)(2,1)}, bf16[7168,256]{1,0:T(8,128)(2,1)}, u32[]{:S(2)}, u32[]{:S(2)}) %collective-permute-start.2) | collective-permute-done | bytes 3670048 | tf_op jit(solution)/shard_map/ppermute | solution.py:11
  199.3 1.0 fusion.11
  200.3 76.1 %collective-permute-done.1 = bf16[7168,256]{1,0:T(8,128)(2,1)} collective-permute-done((bf16[7168,256]{1,0:T(8,128)(2,1)}, bf16[7168,256]{1,0:T(8,128)(2,1)}, u32[]{:S(2)}, u32[]{:S(2)}) %collective-permute-start.1) | collective-permute-done | bytes 3670048 | tf_op jit(solution)/shard_map/ppermute | solution.py:11
  276.5 1.1 multiply_convert_fusion.1
  277.6 2.6 convolution_convert_fusion
  280.2 1.4 fusion.10
  281.6 3.1 fusion.5
  284.7 67.1 %fusion.34 = (bf16[24,7168]{1,0:T(8,128)(2,1)S(1)}, bf16[24,7168]{1,0:T(8,128)(2,1)}, bf16[24,7168]{1,0:T(8,128)(2,1)}, bf16[24,7168]{1,0:T(8,128)(2,1)S(1)}) fusion(bf16[160,7168]{1,0:T(8,128)(2,1)} %convolution_convert_fusion, bf16[160,7168]{1,0:T(8,128)(2,1)} %convolution_convert_fusion.1, bf16[160,7168]{1,0:T(8,128)(2,1)} %fusion.5, ...), kind=kCustom, calls=%all-reduce-scatter.4 | all-reduce-scatter fusion | flops 5505025 | bytes 10551808
  351.8 1.3 collective-permute-start.12
  353.2 1.5 slice.30
  354.7 3.8 collective-permute-start.10
  358.5 7.1 %select_convert_fusion = (bf16[256,7168]{1,0:T(8,128)(2,1)}, f32[256,7168]{1,0:T(8,128)}) fusion(pred[]{:T(512)S(6)} %gt.3, bf16[160,256]{1,0:T(8,128)(2,1)} %copy-done.12, bf16[160,7168]{1,0:T(8,128)(2,1)} %reshape.30), kind=kOutput, calls=%fused_computation.10 | convolution fusion | flops 589037568 | bytes 13385729 | tf_op jit(solution)/shard_map/dot_general | solution.py:26
  365.6 5.5 select_convert_fusion.2
  371.1 2.5 collective-permute-start.13
  373.6 5.3 select_convert_fusion.1
  379.0 2.4 collective-permute-start.16
  381.3 1.5 slice.33
  382.9 3.9 collective-permute-start.14
  387.4 1.9 collective-permute-start.15
  390.1 1.9 collective-permute-start.17
  391.9 7.9 %concatenate.9 = bf16[52,7168]{1,0:T(8,128)(2,1)S(1)} concatenate(bf16[4,7168]{1,0:T(4,128)(2,1)} %copy-done.19, bf16[24,7168]{1,0:T(8,128)(2,1)} %copy-done.11, bf16[24,7168]{1,0:T(8,128)(2,1)} %copy-done.10), dimensions={0} | concatenate | bytes 1490944
  399.8 1.0 broadcast_select_fusion.12
  400.8 1.9 collective-permute-start.11
  402.7 10.1 %collective-permute-start.9 = (bf16[256,7168]{1,0:T(8,128)(2,1)}, bf16[256,7168]{1,0:T(8,128)(2,1)}, u32[]{:S(2)}, u32[]{:S(2)}) collective-permute-start(bf16[256,7168]{1,0:T(8,128)(2,1)} %get-tuple-element.35), channel_id=1, source_target_pairs={{0,64},{8,72},{16,80},{24,88},{32,96},{40,104},{48,112},{56,120},{... | collective-permute-start | bytes 11010056 | tf_op jit(solution)/shard_map/ppermute | solution.py:11
  412.8 7.9 %concatenate.11 = bf16[52,7168]{1,0:T(8,128)(2,1)S(1)} concatenate(bf16[4,7168]{1,0:T(4,128)(2,1)} %collective-permute-done.17, bf16[24,7168]{1,0:T(8,128)(2,1)} %collective-permute-done.16, bf16[24,7168]{1,0:T(8,128)(2,1)} %get-tuple-element.13), dimensions={0} | concatenate | bytes 1490944
  420.7 1.0 broadcast_select_fusion.10
  421.7 3.5 collective-permute-start.8
  425.2 7.9 %concatenate.8 = bf16[52,7168]{1,0:T(8,128)(2,1)S(1)} concatenate(bf16[4,7168]{1,0:T(4,128)(2,1)} %collective-permute-done.11, bf16[24,7168]{1,0:T(8,128)(2,1)} %collective-permute-done.10, bf16[24,7168]{1,0:T(8,128)(2,1)} %get-tuple-element.12), dimensions={0} | concatenate | bytes 1490944
  433.3 3.4 collective-permute-start.6
  436.7 9.5 %concatenate.10 = bf16[52,7168]{1,0:T(8,128)(2,1)} concatenate(bf16[4,7168]{1,0:T(4,128)(2,1)} %collective-permute-done.15, bf16[24,7168]{1,0:T(8,128)(2,1)} %collective-permute-done.14, bf16[24,7168]{1,0:T(8,128)(2,1)S(1)} %get-tuple-element.14), dimensions={0} | concatenate | bytes 1490944
  446.3 1.3 constant_dynamic-slice_fusion
  447.6 210.4 %collective-permute-done.4 = bf16[20,7168]{1,0:T(8,128)(2,1)} collective-permute-done((bf16[20,7168]{1,0:T(8,128)(2,1)}, bf16[20,7168]{1,0:T(8,128)(2,1)}, u32[]{:S(2)}, u32[]{:S(2)}) %collective-permute-start.4) | collective-permute-done | bytes 286752 | tf_op jit(solution)/shard_map/ppermute | solution.py:11
  658.0 2.2 maximum_bitcast_fusion
  660.2 4.2 collective-permute-done.6
  664.3 2.3 maximum_bitcast_fusion.1
  666.7 7.9 %fusion.6 = bf16[1,256,7168]{2,1,0:T(8,128)(2,1)} fusion(bf16[256,7168]{1,0:T(8,128)(2,1)} %collective-permute-done.9, f32[256,7168]{1,0:T(8,128)} %get-tuple-element.36, bf16[160,256]{1,0:T(8,128)(2,1)S(1)} %get-tuple-element.25, bf16[160,7168]{1,0:T(8,128)(2,1)S(1)} %copy-done.9, pred[]{:T(512)S(6)} %gt.3), kind=kOutput, calls=%fused_computation.11 | convolution fusion | flops 596377600 | bytes 17055744 | tf_op jit(solution)/shard_map/dot_general | solution.py:26
  674.6 6.0 fusion.8
  680.6 5.8 fusion.7
  (83 shorter events, 6.9 us)
Async XLA Ops:
  7.2 73.1 %all-gather.9.cloned.1.call-start = ((), (), s32[]{:S(2)}) async-start(), calls=%async_computation.2 | async-start | bytes 3096576 | tf_op jit(solution)/shard_map/all_gather | solution.py:85
  11.8 84.9 %all-gather.11.cloned.1.call-start = ((), (), s32[]{:S(2)}) async-start(), calls=%async_computation.3 | async-start | bytes 3096576 | tf_op jit(solution)/shard_map/all_gather | solution.py:86
  11.8 12.1 %collective-permute-start.5 = (bf16[20,7168]{1,0:T(8,128)(2,1)S(1)}, bf16[20,7168]{1,0:T(8,128)(2,1)S(1)}, u32[]{:S(2)}, u32[]{:S(2)}) collective-permute-start(bf16[20,7168]{1,0:T(8,128)(2,1)S(1)} %get-tuple-element.16), channel_id=1, source_target_pairs={{0,64},{8,72},{16,80},{24,88},{32,96},{40,104},{48,112},{56,120},{... | collective-permute-start | bytes 860168 | tf_op jit(solution)/shard_map/ppermute | solution.py:11
  24.9 10.8 %collective-permute-start = (bf16[20,7168]{1,0:T(8,128)(2,1)S(1)}, bf16[20,7168]{1,0:T(8,128)(2,1)S(1)}, u32[]{:S(2)}, u32[]{:S(2)}) collective-permute-start(bf16[20,7168]{1,0:T(8,128)(2,1)S(1)} %get-tuple-element.18), channel_id=1, source_target_pairs={{0,64},{8,72},{16,80},{24,88},{32,96},{40,104},{48,112},{56,120},{... | collective-permute-start | bytes 860168 | tf_op jit(solution)/shard_map/ppermute | solution.py:11
  30.0 13.1 %copy-start.20 = (u32[128]{0:T(128)S(1)}, u32[128]{0:T(128)}, u32[]{:S(2)}) copy-start(u32[128]{0:T(128)} %constant.32) | copy-start | bytes 1540
  30.0 43.4 %all-to-all-start = ((bf16[8,20,7168]{2,1,0:T(8,128)(2,1)}), bf16[8,20,7168]{2,1,0:T(8,128)(2,1)}, u32[]{:S(2)}, u32[]{:S(2)}) async-start(bf16[8,20,7168]{2,1,0:T(8,128)(2,1)} %stack.2), calls=%async_computation | async-start | bytes 5505024 | tf_op jit(solution)/shard_map/all_to_all | solution.py:52
  34.6 75.2 %all-gather.7.cloned.1.call-start = ((), (), s32[]{:S(2)}) async-start(), calls=%async_computation.1 | async-start | bytes 3096576 | tf_op jit(solution)/shard_map/all_gather | solution.py:84
  36.6 84.1 %collective-permute-start.3 = (bf16[256,7168]{1,0:T(8,128)(2,1)}, bf16[256,7168]{1,0:T(8,128)(2,1)}, u32[]{:S(2)}, u32[]{:S(2)}) collective-permute-start(bf16[256,7168]{1,0:T(8,128)(2,1)} %bitcast.103), channel_id=1, source_target_pairs={{0,64},{8,72},{16,80},{24,88},{32,96},{40,104},{48,112},{56,120},{... | collective-permute-start | bytes 11010056 | tf_op jit(solution)/shard_map/ppermute | solution.py:11
  39.6 159.7 %collective-permute-start.2 = (bf16[7168,256]{1,0:T(8,128)(2,1)}, bf16[7168,256]{1,0:T(8,128)(2,1)}, u32[]{:S(2)}, u32[]{:S(2)}) collective-permute-start(bf16[7168,256]{1,0:T(8,128)(2,1)} %bitcast.102), channel_id=1, source_target_pairs={{0,64},{8,72},{16,80},{24,88},{32,96},{40,104},{48,112},{56,120},{... | collective-permute-start | bytes 11010056 | tf_op jit(solution)/shard_map/ppermute | solution.py:11
  40.2 236.3 %collective-permute-start.1 = (bf16[7168,256]{1,0:T(8,128)(2,1)}, bf16[7168,256]{1,0:T(8,128)(2,1)}, u32[]{:S(2)}, u32[]{:S(2)}) collective-permute-start(bf16[7168,256]{1,0:T(8,128)(2,1)} %bitcast.101), channel_id=1, source_target_pairs={{0,64},{8,72},{16,80},{24,88},{32,96},{40,104},{48,112},{56,120},{... | collective-permute-start | bytes 11010056 | tf_op jit(solution)/shard_map/ppermute | solution.py:11
  76.2 3.3 copy-start.2
  84.5 4.3 copy-start.7
  88.7 2.2 copy-start.13
  88.8 4.3 copy-start.17
  88.8 2.9 copy-start.3
  91.7 2.2 copy-start.5
  114.0 85.4 %copy-start = (bf16[160,7168]{1,0:T(8,128)(2,1)S(1)}, bf16[160,7168]{1,0:T(8,128)(2,1)}, u32[]{:S(2)}) copy-start(bf16[160,7168]{1,0:T(8,128)(2,1)} %reshape.26) | copy-start | bytes 6881284
  114.0 85.4 %copy-start.6 = (bf16[1,7168,256]{2,1,0:T(8,128)(2,1)S(1)}, bf16[1,7168,256]{2,1,0:T(8,128)(2,1)}, u32[]{:S(2)}) copy-start(bf16[1,7168,256]{2,1,0:T(8,128)(2,1)} %param.10) | copy-start | bytes 11010052
  124.6 151.9 %copy-start.4 = (bf16[1,7168,256]{2,1,0:T(8,128)(2,1)S(1)}, bf16[1,7168,256]{2,1,0:T(8,128)(2,1)}, u32[]{:S(2)}) copy-start(bf16[1,7168,256]{2,1,0:T(8,128)(2,1)} %param.9) | copy-start | bytes 11010052
  200.3 77.3 %copy-start.8 = (bf16[1,256,7168]{2,1,0:T(8,128)(2,1)S(1)}, bf16[1,256,7168]{2,1,0:T(8,128)(2,1)}, u32[]{:S(2)}) copy-start(bf16[1,256,7168]{2,1,0:T(8,128)(2,1)} %param.11) | copy-start | bytes 11010052
  277.6 2.6 copy-start.12
  277.6 4.0 copy-start.15
  351.8 13.8 %copy-start.10 = (bf16[24,7168]{1,0:T(8,128)(2,1)}, bf16[24,7168]{1,0:T(8,128)(2,1)S(1)}, u32[]{:S(2)}) copy-start(bf16[24,7168]{1,0:T(8,128)(2,1)S(1)} %get-tuple-element.11) | copy-start | bytes 1032196
  351.8 37.5 %collective-permute-start.12 = (bf16[24,7168]{1,0:T(8,128)(2,1)S(1)}, bf16[24,7168]{1,0:T(8,128)(2,1)S(1)}, u32[]{:S(2)}, u32[]{:S(2)}) collective-permute-start(bf16[24,7168]{1,0:T(8,128)(2,1)S(1)} %get-tuple-element.11), channel_id=1, source_target_pairs={{0,1},{1,2},{2,3},{3,4},{4,5},{5,6},{6,7},{8,9},{9,10},{10,11},{11... | collective-permute-start | bytes 1032200
  354.7 10.9 %copy-start.1 = (bf16[160,7168]{1,0:T(8,128)(2,1)S(1)}, bf16[160,7168]{1,0:T(8,128)(2,1)}, u32[]{:S(2)}) copy-start(bf16[160,7168]{1,0:T(8,128)(2,1)} %reshape.26) | copy-start | bytes 6881284
  354.7 10.9 %copy-start.16 = (bf16[160,256]{1,0:T(8,128)(2,1)S(1)}, bf16[160,256]{1,0:T(8,128)(2,1)}, u32[]{:S(2)}) copy-start(bf16[160,256]{1,0:T(8,128)(2,1)} %copy-done.15) | copy-start | bytes 245764
  354.7 67.0 %collective-permute-start.10 = (bf16[24,7168]{1,0:T(8,128)(2,1)}, bf16[24,7168]{1,0:T(8,128)(2,1)}, u32[]{:S(2)}, u32[]{:S(2)}) collective-permute-start(bf16[24,7168]{1,0:T(8,128)(2,1)} %get-tuple-element.12), channel_id=1, source_target_pairs={{0,1},{1,2},{2,3},{3,4},{4,5},{5,6},{6,7},{8,9},{9,10},{10,11},{11... | collective-permute-start | bytes 1032200
  371.1 16.3 %collective-permute-start.13 = (bf16[4,7168]{1,0:T(4,128)(2,1)S(1)}, bf16[4,7168]{1,0:T(4,128)(2,1)S(1)}, u32[]{:S(2)}, u32[]{:S(2)}) collective-permute-start(bf16[4,7168]{1,0:T(4,128)(2,1)S(1)} %slice.31), channel_id=1, source_target_pairs={{0,2},{1,3},{2,4},{3,5},{4,6},{5,7},{8,10},{9,11},{10,12},{11,13},... | collective-permute-start | bytes 172040
  379.0 23.8 %collective-permute-start.16 = (bf16[24,7168]{1,0:T(8,128)(2,1)}, bf16[24,7168]{1,0:T(8,128)(2,1)}, u32[]{:S(2)}, u32[]{:S(2)}) collective-permute-start(bf16[24,7168]{1,0:T(8,128)(2,1)} %get-tuple-element.13), channel_id=1, source_target_pairs={{0,1},{1,2},{2,3},{3,4},{4,5},{5,6},{6,7},{8,9},{9,10},{10,11},{11... | collective-permute-start | bytes 1032200
  382.9 50.4 %collective-permute-start.14 = (bf16[24,7168]{1,0:T(8,128)(2,1)S(1)}, bf16[24,7168]{1,0:T(8,128)(2,1)}, u32[]{:S(2)}, u32[]{:S(2)}) collective-permute-start(bf16[24,7168]{1,0:T(8,128)(2,1)S(1)} %get-tuple-element.14), channel_id=1, source_target_pairs={{0,1},{1,2},{2,3},{3,4},{4,5},{5,6},{6,7},{8,9},{9,10},{10,11},{11... | collective-permute-start | bytes 1032200
  387.4 1.9 copy-start.19
  387.4 45.7 %collective-permute-start.15 = (bf16[4,7168]{1,0:T(4,128)(2,1)}, bf16[4,7168]{1,0:T(4,128)(2,1)}, u32[]{:S(2)}, u32[]{:S(2)}) collective-permute-start(bf16[4,7168]{1,0:T(4,128)(2,1)} %slice.32), channel_id=1, source_target_pairs={{0,2},{1,3},{2,4},{3,5},{4,6},{5,7},{8,10},{9,11},{10,12},{11,13},... | collective-permute-start | bytes 172040
  389.3 0.7 copy-start.11
  390.1 10.8 %collective-permute-start.17 = (bf16[4,7168]{1,0:T(4,128)(2,1)}, bf16[4,7168]{1,0:T(4,128)(2,1)}, u32[]{:S(2)}, u32[]{:S(2)}) collective-permute-start(bf16[4,7168]{1,0:T(4,128)(2,1)} %slice.33), channel_id=1, source_target_pairs={{0,2},{1,3},{2,4},{3,5},{4,6},{5,7},{8,10},{9,11},{10,12},{11,13},... | collective-permute-start | bytes 172040
  400.8 20.9 %collective-permute-start.11 = (bf16[4,7168]{1,0:T(4,128)(2,1)}, bf16[4,7168]{1,0:T(4,128)(2,1)}, u32[]{:S(2)}, u32[]{:S(2)}) collective-permute-start(bf16[4,7168]{1,0:T(4,128)(2,1)} %slice.30), channel_id=1, source_target_pairs={{0,2},{1,3},{2,4},{3,5},{4,6},{5,7},{8,10},{9,11},{10,12},{11,13},... | collective-permute-start | bytes 172040
  402.7 263.9 %collective-permute-start.9 = (bf16[256,7168]{1,0:T(8,128)(2,1)}, bf16[256,7168]{1,0:T(8,128)(2,1)}, u32[]{:S(2)}, u32[]{:S(2)}) collective-permute-start(bf16[256,7168]{1,0:T(8,128)(2,1)} %get-tuple-element.35), channel_id=1, source_target_pairs={{0,64},{8,72},{16,80},{24,88},{32,96},{40,104},{48,112},{56,120},{... | collective-permute-start | bytes 11010056 | tf_op jit(solution)/shard_map/ppermute | solution.py:11
  421.7 252.9 %collective-permute-start.7 = (bf16[7168,256]{1,0:T(8,128)(2,1)}, bf16[7168,256]{1,0:T(8,128)(2,1)}, u32[]{:S(2)}, u32[]{:S(2)}) collective-permute-start(bf16[7168,256]{1,0:T(8,128)(2,1)} %get-tuple-element.31), channel_id=1, source_target_pairs={{0,64},{8,72},{16,80},{24,88},{32,96},{40,104},{48,112},{56,120},{... | collective-permute-start | bytes 11010056 | tf_op jit(solution)/shard_map/ppermute | solution.py:11
  421.7 258.9 %collective-permute-start.8 = (bf16[7168,256]{1,0:T(8,128)(2,1)}, bf16[7168,256]{1,0:T(8,128)(2,1)}, u32[]{:S(2)}, u32[]{:S(2)}) collective-permute-start(bf16[7168,256]{1,0:T(8,128)(2,1)} %get-tuple-element.33), channel_id=1, source_target_pairs={{0,64},{8,72},{16,80},{24,88},{32,96},{40,104},{48,112},{56,120},{... | collective-permute-start | bytes 11010056 | tf_op jit(solution)/shard_map/ppermute | solution.py:11
  433.1 224.9 %collective-permute-start.4 = (bf16[20,7168]{1,0:T(8,128)(2,1)}, bf16[20,7168]{1,0:T(8,128)(2,1)}, u32[]{:S(2)}, u32[]{:S(2)}) collective-permute-start(bf16[20,7168]{1,0:T(8,128)(2,1)} %get-tuple-element.22), channel_id=1, source_target_pairs={{0,64},{8,72},{16,80},{24,88},{32,96},{40,104},{48,112},{56,120},{... | collective-permute-start | bytes 860168 | tf_op jit(solution)/shard_map/ppermute | solution.py:11
  433.3 231.1 %collective-permute-start.6 = (bf16[20,7168]{1,0:T(8,128)(2,1)}, bf16[20,7168]{1,0:T(8,128)(2,1)}, u32[]{:S(2)}, u32[]{:S(2)}) collective-permute-start(bf16[20,7168]{1,0:T(8,128)(2,1)} %get-tuple-element.20), channel_id=1, source_target_pairs={{0,64},{8,72},{16,80},{24,88},{32,96},{40,104},{48,112},{56,120},{... | collective-permute-start | bytes 860168 | tf_op jit(solution)/shard_map/ppermute | solution.py:11
  446.2 220.4 %copy-start.9 = (bf16[160,7168]{1,0:T(8,128)(2,1)S(1)}, bf16[160,7168]{1,0:T(8,128)(2,1)}, u32[]{:S(2)}) copy-start(bf16[160,7168]{1,0:T(8,128)(2,1)} %reshape.28) | copy-start | bytes 6881284
  664.3 10.2 %slice-start.2 = ((s8[7340032]{0:T(1024)(128)(4,1)}), s8[4194304]{0:T(1024)(128)(4,1)S(1)}, s32[]{:S(2)}) async-start(s8[7340032]{0:T(1024)(128)(4,1)} %bitcast.99), calls=%async_computation.6 | async-start | bytes 8388608
  666.7 7.9 %slice-start.3 = ((s8[7340032]{0:T(1024)(128)(4,1)}), s8[3145728]{0:T(1024)(128)(4,1)S(1)}, s32[]{:S(2)}) async-start(s8[7340032]{0:T(1024)(128)(4,1)} %bitcast.99), calls=%async_computation.7 | async-start | bytes 6291456
  666.7 7.9 %copy-start.14 = (bf16[160,256]{1,0:T(8,128)(2,1)S(1)}, bf16[160,256]{1,0:T(8,128)(2,1)}, u32[]{:S(2)}) copy-start(bf16[160,256]{1,0:T(8,128)(2,1)} %copy-done.13) | copy-start | bytes 245764
  666.7 13.9 %slice-start = ((s8[7340032]{0:T(1024)(128)(4,1)}), s8[4194304]{0:T(1024)(128)(4,1)S(1)}, s32[]{:S(2)}) async-start(s8[7340032]{0:T(1024)(128)(4,1)} %bitcast.97), calls=%async_computation.4 | async-start | bytes 8388608
  674.6 6.0 slice-start.1
  674.6 6.0 copy-start.18
Sparse Core Ops, SparseCore 0:
  11.9 29.1 all-gather.8
  43.3 38.1 all-gather.10
  83.7 26.0 all-gather.6
